TPU v7x, 256 devices: a whole 4x4x8 slice. The times are simulated.
256 devices in a mesh: kv: 8 (over x, core), seq: 32 (over z, y).
Axes of the slice: x: 4, y: 4, z: 8, core: 2. Of those that a mesh axis runs over, the one named last changes fastest.
Arguments:
- hidden_states: bfloat16 [6144, 2048], P('seq')
- attn_gain: float32 [2048], replicated, may hold values from 0.5 to 1.5
- w_q: bfloat16 [2048, 2048], P(None, 'kv')
- w_k: bfloat16 [2048, 512], P(None, 'kv')
- w_v: bfloat16 [2048, 512], P(None, 'kv'), may hold values from -0.125 to 0.125
- w_o: bfloat16 [2048, 2048], P('kv'), may hold values from -0.125 to 0.125
- final_gain: float32 [2048], replicated, may hold values from 0.5 to 1.5
- w_head: bfloat16 [2048, 49408], P(None, ('kv', 'seq'))
- doc_lengths: int32 [26], replicated, may hold values from 1 to 3072, as said below
- target_ids: int32 [6144], replicated, may hold values from 0 to 49154, as said below
- vocab_mask: int32 [49408], P(('kv', 'seq')), may hold values from 0 to 1, as said below
Outputs:
- log_probs: float32 [6144], P('seq')
- entropies: float32 [6144], P('seq')
Inputs may be any that keep to these rules, and one draw needn't show every extreme that they name: `doc_lengths`: they sum to 6144; one is 3072, one more is over 1536, every other is under 64. `target_ids`: each names an entry whose vocab_mask is 1. `vocab_mask`: entries from 49155 on are 0.
All inputs are finite; a program needn't handle non-finite values.
Results may differ from a plain program's by a relative error of at most 0.0045.
Values may be sent and summed in bfloat16 or wider, within the bound.
No kernel may reach another device: no remote copies, remote signals or barrier semaphores. Data moves between devices by JAX's collectives and lax.ppermute only.
A program may use at most 128 MiB of HBM per device.

v0:
```python
import math
import jax
import jax.numpy as jnp
from jax import lax
from jax.sharding import Mesh, PartitionSpec as P

HEAD_DIM = 64
ROPE_THETA = 10000000.0
NORM_EPS = 1e-05
NEG_FILL = -1e30
ATTN_SCALE = 0.015625
RESID_SCALE = 5.0
LOGIT_SCALE = 0.125


def rms_norm(values, gain_vec):
    return (
        values * lax.rsqrt(jnp.mean(values * values, axis=-1, keepdims=True) + NORM_EPS) * gain_vec
    )


def rotate(values, positions):
    half_dim = values.shape[-1] // 2
    inverse = jnp.exp(
        jnp.arange(half_dim, dtype=jnp.float32) * (-2.0 * math.log(ROPE_THETA) / values.shape[-1])
    )
    angles = positions.astype(jnp.float32)[:, None] * inverse[None, :]
    cos_val = jnp.cos(angles)[:, None, :]
    sine_val = jnp.sin(angles)[:, None, :]
    lower_half = values[..., :half_dim]
    upper_half = values[..., half_dim:]
    return jnp.concatenate(
        [
            lower_half * cos_val - upper_half * sine_val,
            upper_half * cos_val + lower_half * sine_val,
        ],
        axis=-1,
    )


def local(
    hidden_states,
    attn_gain,
    w_q,
    w_k,
    w_v,
    w_o,
    final_gain,
    w_head,
    doc_lengths,
    target_ids,
    vocab_mask,
):
    tok_rows = hidden_states.shape[0]
    seq_index = lax.axis_index(("z", "y"))
    kv_local = w_k.shape[1] // HEAD_DIM
    q_local = w_q.shape[1] // HEAD_DIM
    group_size = q_local // kv_local
    key_width = kv_local * HEAD_DIM
    stream = hidden_states.astype(jnp.float32)
    normed_in = rms_norm(stream, attn_gain).astype(jnp.bfloat16)
    queries = jnp.dot(normed_in, w_q, preferred_element_type=jnp.float32)
    key_proj = jnp.dot(normed_in, w_k, preferred_element_type=jnp.float32)
    value_proj = jnp.dot(normed_in, w_v, preferred_element_type=jnp.float32)
    token_pos = seq_index * tok_rows + jnp.arange(tok_rows, dtype=jnp.int32)
    doc_ends = jnp.cumsum(doc_lengths)
    doc_starts = doc_ends - doc_lengths
    doc_start = jnp.max(
        jnp.where(doc_starts[None, :] <= token_pos[:, None], doc_starts[None, :], 0), axis=1
    )
    positions = token_pos - doc_start
    rotated_q = rotate(queries.reshape(tok_rows, q_local, HEAD_DIM), positions).astype(jnp.bfloat16)
    rotated_q = rotated_q.reshape(tok_rows, kv_local, group_size, HEAD_DIM)
    rotated_k = rotate(key_proj.reshape(tok_rows, kv_local, HEAD_DIM), positions).astype(
        jnp.bfloat16
    )
    packed = jnp.concatenate(
        [rotated_k.reshape(tok_rows, key_width), value_proj.astype(jnp.bfloat16)], axis=1
    )
    earliest = doc_start[0]
    latest = token_pos[tok_rows - 1]
    initial = (
        jnp.full((kv_local, group_size, tok_rows), NEG_FILL, jnp.float32),
        jnp.zeros((kv_local, group_size, tok_rows), jnp.float32),
        jnp.zeros((kv_local, group_size, tok_rows, HEAD_DIM), jnp.float32),
    )
    shard_rows = lax.all_gather(packed, ("z", "y"), axis=0, tiled=True)
    offset = jnp.int32(0)
    row_count = shard_rows.shape[0]
    key_pos = jnp.arange(row_count, dtype=jnp.int32)

    def update(current):
        top_score, totals, context_sum = current
        key_rows = shard_rows[:, :key_width].reshape(row_count, kv_local, HEAD_DIM)
        value_rows = shard_rows[:, key_width:].reshape(row_count, kv_local, HEAD_DIM)
        scores = (
            jnp.einsum("tkgd,skd->kgts", rotated_q, key_rows, preferred_element_type=jnp.float32)
            * ATTN_SCALE
        )
        allowed = (key_pos[None, :] >= doc_start[:, None]) & (
            key_pos[None, :] <= token_pos[:, None]
        )
        scores = jnp.where(allowed, scores, NEG_FILL)
        new_top = jnp.maximum(top_score, jnp.max(scores, axis=-1))
        weights = jnp.where(allowed, jnp.exp(scores - new_top[..., None]), 0.0)
        rescale = jnp.exp(top_score - new_top)
        totals = jnp.sum(weights, axis=-1)
        context_sum = jnp.einsum(
            "kgts,skd->kgtd",
            weights.astype(jnp.bfloat16),
            value_rows,
            preferred_element_type=jnp.float32,
        )
        return (new_top, totals, context_sum)

    skip_piece = (offset + row_count <= earliest) | (offset > latest)
    top_score, totals, context_sum = lax.cond(skip_piece, lambda current: current, update, initial)
    context = (
        (context_sum / totals[..., None])
        .transpose(2, 0, 1, 3)
        .reshape(tok_rows, q_local * HEAD_DIM)
        .astype(jnp.bfloat16)
    )
    vocab_local = w_head.shape[1]
    y_count = lax.psum(1, "y")
    z_count = lax.psum(1, "z")
    z_index = lax.axis_index("z")
    y_index = lax.axis_index("y")
    kv_index = lax.axis_index("kv")
    attn_out = lax.psum(jnp.dot(context, w_o, preferred_element_type=jnp.float32), "kv")
    final_in = rms_norm(stream + RESID_SCALE * attn_out, final_gain).astype(jnp.bfloat16)
    head_rows = lax.all_gather(final_in, "y", axis=0, tiled=True)
    group_rows = head_rows.shape[0]
    head_cols = lax.all_gather(w_head, "z", axis=1, tiled=True)
    mask_cols = lax.all_gather(vocab_mask, "z", axis=0, tiled=True)
    live_mask = mask_cols == 1
    shard_ids = (
        kv_index * (z_count * y_count) + jnp.arange(z_count, dtype=jnp.int32) * y_count + y_index
    )
    columns = (
        shard_ids[:, None] * vocab_local + jnp.arange(vocab_local, dtype=jnp.int32)[None, :]
    ).reshape(-1)
    row_ids = lax.dynamic_slice_in_dim(target_ids, z_index * group_rows, group_rows, 0)
    logits = jnp.dot(head_rows, head_cols, preferred_element_type=jnp.float32) * LOGIT_SCALE
    masked = jnp.where(live_mask[None, :], logits, NEG_FILL)
    top_row = jnp.max(masked, axis=1)
    shifted = jnp.where(live_mask[None, :], masked - top_row[:, None], 0.0)
    expw = jnp.where(live_mask[None, :], jnp.exp(shifted), 0.0)
    target = jnp.sum(jnp.where(row_ids[:, None] == columns[None, :], logits, 0.0), axis=1)
    row_stats = jnp.stack([top_row, jnp.sum(expw, axis=1), jnp.sum(expw * shifted, axis=1), target])
    top_all = lax.pmax(row_stats[0], ("kv", "y"))
    rescale = jnp.exp(row_stats[0] - top_all)
    total_all, spread_all, target_all = lax.psum(
        (
            row_stats[1] * rescale,
            rescale * (row_stats[2] + (row_stats[0] - top_all) * row_stats[1]),
            row_stats[3],
        ),
        ("kv", "y"),
    )
    log_prob = target_all - top_all - jnp.log(total_all)
    entropy = jnp.log(total_all) - spread_all / total_all
    log_probs = lax.dynamic_slice_in_dim(log_prob, y_index * tok_rows, tok_rows, 0)
    entropies = lax.dynamic_slice_in_dim(entropy, y_index * tok_rows, tok_rows, 0)
    return (log_probs, entropies)


def solution(mesh):
    kv_size, seq_size = mesh.devices.shape
    z_size = mesh.shape["seq"] // 4 if mesh.shape["seq"] % 4 == 0 else mesh.shape["seq"]
    y_size = seq_size // z_size
    split_mesh = Mesh(mesh.devices.reshape(kv_size, z_size, y_size), ("kv", "z", "y"))
    seq = ("z", "y")
    in_specs = (
        P(seq, None),
        P(),
        P(None, "kv"),
        P(None, "kv"),
        P(None, "kv"),
        P("kv", None),
        P(),
        P(None, ("kv",) + seq),
        P(),
        P(),
        P(("kv",) + seq),
    )
    out_specs = (P(seq), P(seq))
    return jax.shard_map(
        local, mesh=split_mesh, in_specs=in_specs, out_specs=out_specs, check_vma=False
    )
```

profile of v0, /device:TPU:32, one launch (start us, length us, event | category | flops | bytes accessed | tf_op | source)
XLA Modules:
  0.0 449.0 jit_solution(1061210086343181944)
XLA Ops:
  8.1 0.9 copy.22
  10.0 1.4 fusion.16
  11.3 1.6 convolution_bitcast_fusion
  13.0 1.6 convolution_convert_fusion
  14.9 0.7 copy.23
  19.0 75.5 %all-gather.5.cloned.1.call-done = bf16[6144,128]{1,0:T(8,128)(2,1)} async-done(((bf16[192,128]{1,0:T(8,128)(2,1)}), bf16[6144,128]{1,0:T(8,128)(2,1)}) %all-gather.5.cloned.1.call-update) | async-done | bytes 1572880 | tf_op jit(solution)/shard_map/all_gather | solution.py:87
  94.5 21.4 %conditional.1 = (f32[1,4,192]{2,1,0:T(4,128)S(1)}, f32[1,4,192,64]{2,3,1,0:T(8,128)S(1)}) conditional(s32[]{:T(128)} %bitcast.9, (s32[6144]{0:T(1024)S(1)}, s32[6144]{0:T(1024)S(1)}, s32[192]{0:T(256)S(1)}, s32[192]{0:T(256)S(1)}, bf16[6144,128]{1,0:T(8,128)(2,1)}, /*index=5*/bf16[192,1,4,64]{0,3,2,1:T(8,128)(2,1)S(1)}) %tuple.16, () %tuple.17), branch_computations={%region_3.6_spmd, %region_6.7_spmd} | conditional | flops 1272839424 | bytes 66424336 | solution.py:117
  94.5 1.0 compare_and_fusion
  95.5 2.6 copy.25
  98.1 5.0 %fusion = (f32[4,192]{1,0:T(4,128)S(1)}, f32[6144,192,4]{0,1,2:T(8,128)S(1)}) fusion(pred[192,6144]{1,0:T(8,128)(4,1)S(1)} %compare_and_fusion, bf16[192,1,4,64]{0,3,2,1:T(8,128)(2,1)S(1)} %get-tuple-element.16, bf16[6144,128]{0,1:T(8,128)(2,1)} %copy.25), kind=kOutput, calls=%fused_computation.2 | convolution fusion | flops 618134784 | bytes 20941824 | tf_op jit(solution)/shard_map/cond/branch_0_fun/tkgd,skd->kgts/dot_general | solution.py:97
  103.1 6.3 %fusion.7 = f32[1,4,192,64]{2,3,1,0:T(8,128)S(1)} fusion(f32[6144,192,4]{0,1,2:T(8,128)S(1)} %get-tuple-element.42, f32[4,192]{1,0:T(4,128)S(1)} %broadcast_maximum_fusion, pred[192,6144]{1,0:T(8,128)(4,1)S(1)} %compare_and_fusion, bf16[6144,128]{0,1:T(8,128)(2,1)} %copy.25), kind=kOutput, calls=%fused_computation.9 | convolution fusion | flops 627572736 | bytes 21040128 | tf_op jit(solution)/shard_map/cond/branch_0_fun/kgts,skd->kgtd/dot_general | solution.py:108
  109.4 6.5 %fusion.2 = f32[4,192]{1,0:T(4,128)S(1)} fusion(f32[6144,192,4]{0,1,2:T(8,128)S(1)} %get-tuple-element.42, f32[4,192]{1,0:T(4,128)S(1)} %broadcast_maximum_fusion, pred[192,6144]{1,0:T(8,128)(4,1)S(1)} %compare_and_fusion), kind=kLoop, calls=%fused_computation.4 | loop fusion | flops 23592192 | bytes 20060160 | tf_op jit(solution)/shard_map/cond/branch_0_fun/reduce_sum | solution.py:107
  115.9 1.6 fusion.35
  118.4 67.6 %all-reduce.4.cloned.1.call-done = f32[192,2048]{1,0:T(8,128)} async-done(((f32[192,2048]{1,0:T(8,128)}), f32[192,2048]{1,0:T(8,128)}) %all-reduce.4.cloned.1.call-update) | async-done | bytes 1572880 | tf_op jit(solution)/shard_map/psum | solution.py:130
  186.1 1.7 multiply_reduce_fusion.1
  187.8 2.6 multiply_convert_fusion
  191.9 0.8 dynamic_slice.9
  192.9 14.0 %all-reduce = s32[1544]{0:T(1024)S(1)} all-reduce(s32[1544]{0:T(1024)S(1)} %dynamic-update-slice), channel_id=1, replica_groups=mesh['kv'=8,'z'=8,'y'=4] {'z'}, use_global_device_ids=true, to_apply=%add | all-reduce | flops 1544 | bytes 12352
  207.0 7.8 %reshape.284 = bf16[1544,2048]{1,0:T(8,128)(2,1)} reshape(bf16[8,193,2048]{2,1,0:T(8,128)(2,1)} %all-gather.9.cloned.1.call-done) | data formatting | bytes 12648448
  214.8 22.4 %all-gather.7.cloned.1.call-done = bf16[768,2048]{1,0:T(8,128)(2,1)} async-done(((bf16[192,2048]{1,0:T(8,128)(2,1)}), bf16[768,2048]{1,0:T(8,128)(2,1)}) %all-gather.7.cloned.1.call-update) | async-done | bytes 3145744 | tf_op jit(solution)/shard_map/all_gather | solution.py:132
  237.2 9.8 %select_reduce_fusion.1 = (f32[768]{0:T(1024)S(1)}, f32[768,1544]{0,1:T(8,128)}) fusion(pred[1544]{0:T(1024)(128)(4,1)S(1)} %broadcast_compare_fusion, bf16[768,2048]{1,0:T(8,128)(2,1)} %all-gather.7.cloned.1.call-done, bf16[1544,2048]{1,0:T(8,128)(2,1)} %reshape.284), kind=kOutput, calls=%fused_computation.23 | convolution fusion | flops 4860560384 | bytes 14217736 | tf_op jit(solution)/shard_map/dot_general | solution.py:144
  247.0 64.9 %pmax.7 = f32[768]{0:T(1024)S(1)} all-reduce(f32[768]{0:T(1024)S(1)} %get-tuple-element.53), channel_id=1, replica_groups=mesh['kv'=8,'z'=8,'y'=4] {'kv','y'}, use_global_device_ids=true, to_apply=%region_12.13 | all-reduce | flops 768 | bytes 6144 | tf_op jit(solution)/shard_map/pmax | solution.py:151
  311.9 4.5 %multiply_reduce_fusion = (f32[768]{0:T(1024)S(1)}, f32[768]{0:T(1024)S(1)}, f32[768]{0:T(1024)S(1)}) fusion(f32[768,1544]{0,1:T(8,128)} %get-tuple-element.54, f32[768]{0:T(1024)S(1)} %get-tuple-element.53, pred[1544]{0:T(1024)(128)(4,1)S(1)} %broadcast_compare_fusion, s32[1544]{0:T(1024)S(1)} %add.107, s32[768]{0:T(1024)S(1)} %dynamic_slice.9), kind=kLoop, calls=%fused_computation.18 | loop fusion | flops 13041408 | bytes 4766248 | tf_op jit(solution)/shard_map/reduce_sum | solution.py:150
  316.5 123.8 %all-reduce.1 = (f32[768]{0:T(1024)S(1)}, f32[768]{0:T(1024)S(1)}, f32[768]{0:T(1024)S(1)}) all-reduce(f32[768]{0:T(1024)S(1)} %get-tuple-element.37, f32[768]{0:T(1024)S(1)} %get-tuple-element.48, f32[768]{0:T(1024)S(1)} %get-tuple-element.47), channel_id=1, replica_groups=mesh['kv'=8,'z'=8,'y'=4] {'kv','y'}, use_global_device_ids=true, to_apply=%region_10.11 | all-reduce | flops 2304 | bytes 18432 | tf_op jit(solution)/shard_map/psum | solution.py:153
  (54 shorter events, 6.4 us)
Async XLA Ops:
  8.0 107.9 %copy-start = (bf16[256,2048]{1,0:T(8,128)(2,1)S(1)}, bf16[256,2048]{1,0:T(8,128)(2,1)}, u32[]{:S(2)}) copy-start(bf16[256,2048]{1,0:T(8,128)(2,1)} %param.18) | copy-start | bytes 3145732
  8.0 10.3 %copy-start.1 = (bf16[192,2048]{1,0:T(8,128)(2,1)S(1)}, bf16[192,2048]{1,0:T(8,128)(2,1)}, u32[]{:S(2)}) copy-start(bf16[192,2048]{1,0:T(8,128)(2,1)} %param.13) | copy-start | bytes 2359300
  8.0 10.3 %copy-start.5 = (f32[2048]{0:T(1024)S(1)}, f32[2048]{0:T(1024)}, u32[]{:S(2)}) copy-start(f32[2048]{0:T(1024)} %param.14) | copy-start | bytes 24580
  8.0 10.3 %copy-start.4 = (bf16[2048,256]{1,0:T(8,128)(2,1)S(1)}, bf16[2048,256]{1,0:T(8,128)(2,1)}, u32[]{:S(2)}) copy-start(bf16[2048,256]{1,0:T(8,128)(2,1)} %param.15) | copy-start | bytes 3145732
  8.0 86.5 %all-gather.5.cloned.1.call-start = ((), (), s32[]{:S(2)}) async-start(), calls=%async_computation | async-start | bytes 1622016 | tf_op jit(solution)/shard_map/all_gather | solution.py:87
  15.6 170.5 %all-reduce.4.cloned.1.call-start = ((), (), s32[]{:S(2)}) async-start(), calls=%async_computation.1 | async-start | bytes 3145728 | tf_op jit(solution)/shard_map/psum | solution.py:130
  115.9 72.0 %copy-start.2 = (f32[2048]{0:T(1024)S(1)}, f32[2048]{0:T(1024)}, u32[]{:S(2)}) copy-start(f32[2048]{0:T(1024)} %param.19) | copy-start | bytes 24580
  117.6 73.1 %copy-start.6 = (u32[256]{0:T(256)S(1)}, u32[256]{0:T(256)}, u32[]{:S(2)}) copy-start(u32[256]{0:T(256)} %constant.73) | copy-start | bytes 3076
  117.6 75.1 %copy-start.3 = (s32[193]{0:T(256)S(1)}, s32[193]{0:T(256)}, u32[]{:S(2)}) copy-start(s32[193]{0:T(256)} %param.23) | copy-start | bytes 2320
  117.6 89.4 %all-gather.9.cloned.1.call-start = ((), (), s32[]{:S(2)}) async-start(), calls=%async_computation.3 | async-start | bytes 7372800 | tf_op jit(solution)/shard_map/all_gather | solution.py:134
  118.2 119.0 %all-gather.7.cloned.1.call-start = ((), (), s32[]{:S(2)}) async-start(), calls=%async_computation.2 | async-start | bytes 3932160 | tf_op jit(solution)/shard_map/all_gather | solution.py:132
Sparse Core Ops, SparseCore 0:
  15.7 78.7 all-gather.4
  117.7 68.2 all-reduce.3
Sparse Core Ops, SparseCore 1:
  119.9 73.3 all-gather.8
  194.9 42.3 all-gather.6
where the time goes:
time: 450 us; the launch traced here: 449 us
  blocking collectives  203 us (45%)
  waiting for transfers between devices  166 us (37%)
  matrix products  26.6 us (6%)
  other arithmetic  19.3 us (4%)
  between operations  17.7 us (4%)
  local copies, waits for them, and re-layouts  16.2 us (4%)
    psum x1, blocking collectives, local(): lax.psum((row_stats[1] * rescale, rescale * (row_stats[2] + (row_stats[0]...  124 us
    all_gather x1, waiting for transfers between devices, local(): shard_rows = lax.all_gather(packed, ('z', 'y'), axis=0, tiled=True)  75.5 us
    psum x1, waiting for transfers between devices, local(): lax.psum(jnp.dot(context, w_o, preferred_element_type=jnp.float32), 'kv')  67.6 us
    pmax x1, blocking collectives, local(): top_all = lax.pmax(row_stats[0], ('kv', 'y'))  64.9 us
    all_gather x1, waiting for transfers between devices, local(): head_rows = lax.all_gather(final_in, 'y', axis=0, tiled=True)  22.4 us
    unnamed x1, blocking collectives  14 us
    dot_general x1, matrix products, local(): jnp.dot(head_rows, head_cols, preferred_element_type=jnp.float32)  9.77 us
  transfers between devices with their start and end apart: 4, of which 3 were waited for; matrix products, arithmetic and copies ran while one was open for 4% of the time, Pallas kernels for 0%

commit v1 on v0

--- a/solution.py
+++ b/solution.py
@@ -127,7 +127,9 @@
     z_index = lax.axis_index("z")
     y_index = lax.axis_index("y")
     kv_index = lax.axis_index("kv")
-    attn_out = lax.psum(jnp.dot(context, w_o, preferred_element_type=jnp.float32), "kv")
+    attn_out = jnp.sum(
+        lax.all_gather(jnp.dot(context, w_o, preferred_element_type=jnp.float32), "kv"), axis=0
+    )
     final_in = rms_norm(stream + RESID_SCALE * attn_out, final_gain).astype(jnp.bfloat16)
     head_rows = lax.all_gather(final_in, "y", axis=0, tiled=True)
     group_rows = head_rows.shape[0]

time: 450 us -> 518 us (1.15)
  waiting for transfers between devices: 166 us -> 234 us
    psum x1 -> x0, waiting for transfers between devices: 67.6 us -> none  [local(): lax.psum(jnp.dot(context, w_o, preferred_element_type=jnp.float32), 'kv')]
    all_gather x0 -> x1, waiting for transfers between devices: none -> 67.2 us  [local(): lax.all_gather(jnp.dot(context, w_o, preferred_element_type=jnp.float32),...]
    all_gather x1, waiting for transfers between devices: 0.03 us -> 54.2 us  [local(): head_cols = lax.all_gather(w_head, 'z', axis=1, tiled=True)]
    all_gather x1, waiting for transfers between devices: 22.4 us -> 36.5 us  [local(): head_rows = lax.all_gather(final_in, 'y', axis=0, tiled=True)]
    reduce_sum x0 -> x1, other arithmetic: none -> 6.03 us  [local(): jnp.sum(lax.all_gather(jnp.dot(context, w_o, preferred_element_type=jnp.f...]
  transfers between devices with their start and end apart: 4 -> 4, of which waited for: 3 -> 4; matrix products, arithmetic and copies ran while one was open for 4% -> 4% of each run, Pallas kernels for 0% -> 0%
where the time goes in v1:
time: 518 us
  waiting for transfers between devices  234 us (45%)
  blocking collectives  203 us (39%)
  matrix products  26.6 us (5%)
  other arithmetic  22.5 us (4%)
  between operations  16 us (3%)
  local copies, waits for them, and re-layouts  15.7 us (3%)
    psum x1, blocking collectives, local(): lax.psum((row_stats[1] * rescale, rescale * (row_stats[2] + (row_stats[0]...  124 us
    all_gather x1, waiting for transfers between devices, local(): shard_rows = lax.all_gather(packed, ('z', 'y'), axis=0, tiled=True)  75.5 us
    all_gather x1, waiting for transfers between devices, local(): lax.all_gather(jnp.dot(context, w_o, preferred_element_type=jnp.float32),...  67.2 us
    pmax x1, blocking collectives, local(): top_all = lax.pmax(row_stats[0], ('kv', 'y'))  65 us
    all_gather x1, waiting for transfers between devices, local(): head_cols = lax.all_gather(w_head, 'z', axis=1, tiled=True)  54.2 us
    all_gather x1, waiting for transfers between devices, local(): head_rows = lax.all_gather(final_in, 'y', axis=0, tiled=True)  36.5 us
    unnamed x1, blocking collectives  13.8 us
  transfers between devices with their start and end apart: 4, of which 4 were waited for; matrix products, arithmetic and copies ran while one was open for 4% of the time, Pallas kernels for 0%

profile of v1, /device:TPU:32, one launch (start us, length us, event | category | flops | bytes accessed | tf_op | source)
XLA Modules:
  0.0 517.7 jit_solution(13739986480736484651)
XLA Ops:
  7.3 0.9 copy.22
  9.1 1.4 fusion.16
  10.5 1.6 convolution_bitcast_fusion
  12.2 1.6 convolution_convert_fusion
  18.2 75.5 %all-gather.7.cloned.1.call-done = bf16[6144,128]{1,0:T(8,128)(2,1)} async-done(((bf16[192,128]{1,0:T(8,128)(2,1)}), bf16[6144,128]{1,0:T(8,128)(2,1)}) %all-gather.7.cloned.1.call-update) | async-done | bytes 1572880 | tf_op jit(solution)/shard_map/all_gather | solution.py:87
  93.7 21.4 %conditional.1 = (f32[1,4,192]{2,1,0:T(4,128)S(1)}, f32[1,4,192,64]{2,3,1,0:T(8,128)S(1)}) conditional(s32[]{:T(128)} %bitcast.9, (s32[6144]{0:T(1024)S(1)}, s32[6144]{0:T(1024)S(1)}, s32[192]{0:T(256)S(1)}, s32[192]{0:T(256)S(1)}, bf16[6144,128]{1,0:T(8,128)(2,1)}, /*index=5*/bf16[192,1,4,64]{0,3,2,1:T(8,128)(2,1)S(1)}) %tuple.16, () %tuple.17), branch_computations={%region_3.6_spmd, %region_6.7_spmd} | conditional | flops 1272839424 | bytes 66424336 | solution.py:117
  93.7 1.0 compare_and_fusion
  94.7 2.6 copy.25
  97.3 5.0 fusion
  102.3 6.3 %fusion.7 = f32[1,4,192,64]{2,3,1,0:T(8,128)S(1)} fusion(f32[6144,192,4]{0,1,2:T(8,128)S(1)} %get-tuple-element.42, f32[4,192]{1,0:T(4,128)S(1)} %broadcast_maximum_fusion, pred[192,6144]{1,0:T(8,128)(4,1)S(1)} %compare_and_fusion, bf16[6144,128]{0,1:T(8,128)(2,1)} %copy.25), kind=kOutput, calls=%fused_computation.9 | convolution fusion | flops 627572736 | bytes 21040128 | tf_op jit(solution)/shard_map/cond/branch_0_fun/kgts,skd->kgtd/dot_general | solution.py:108
  108.6 6.5 %fusion.2 = f32[4,192]{1,0:T(4,128)S(1)} fusion(f32[6144,192,4]{0,1,2:T(8,128)S(1)} %get-tuple-element.42, f32[4,192]{1,0:T(4,128)S(1)} %broadcast_maximum_fusion, pred[192,6144]{1,0:T(8,128)(4,1)S(1)} %compare_and_fusion), kind=kLoop, calls=%fused_computation.4 | loop fusion | flops 23592192 | bytes 20060160 | tf_op jit(solution)/shard_map/cond/branch_0_fun/reduce_sum | solution.py:107
  115.1 1.6 fusion.35
  117.7 67.2 %all-gather.11.cloned.1.call-done = f32[1536,2048]{1,0:T(8,128)} async-done(((f32[192,2048]{1,0:T(8,128)}), f32[1536,2048]{1,0:T(8,128)}) %all-gather.11.cloned.1.call-update) | async-done | bytes 12582928 | tf_op jit(solution)/shard_map/all_gather | solution.py:131
  184.9 6.0 %reduce_sum.66 = f32[192,2048]{1,0:T(8,128)S(1)} reduce(f32[8,192,2048]{2,1,0:T(8,128)} %bitcast.67, f32[]{:T(128)} %constant.60.clone.1), dimensions={0}, to_apply=%region_7.8 | reduce | flops 2752512 | bytes 14155780 | tf_op jit(solution)/shard_map/reduce_sum | solution.py:130
  191.3 1.2 multiply_convert_fusion
  194.0 0.8 dynamic_slice.9
  195.0 13.8 %all-reduce = s32[1544]{0:T(1024)S(1)} all-reduce(s32[1544]{0:T(1024)S(1)} %dynamic-update-slice), channel_id=1, replica_groups=mesh['kv'=8,'z'=8,'y'=4] {'z'}, use_global_device_ids=true, to_apply=%add | all-reduce | flops 1544 | bytes 12352
  208.8 54.2 %all-gather.13.cloned.1.call-done = bf16[8,193,2048]{2,1,0:T(8,128)(2,1)} async-done(((bf16[1,193,2048]{2,1,0:T(8,128)(2,1)}), bf16[8,193,2048]{2,1,0:T(8,128)(2,1)}) %all-gather.13.cloned.1.call-update) | async-done | bytes 6324240 | tf_op jit(solution)/shard_map/all_gather | solution.py:136
  262.9 7.4 %reshape.285 = bf16[1544,2048]{1,0:T(8,128)(2,1)} reshape(bf16[8,193,2048]{2,1,0:T(8,128)(2,1)} %all-gather.13.cloned.1.call-done) | data formatting | bytes 12648448
  270.3 36.5 %all-gather.9.cloned.1.call-done = bf16[768,2048]{1,0:T(8,128)(2,1)} async-done(((bf16[192,2048]{1,0:T(8,128)(2,1)}), bf16[768,2048]{1,0:T(8,128)(2,1)}) %all-gather.9.cloned.1.call-update) | async-done | bytes 3145744 | tf_op jit(solution)/shard_map/all_gather | solution.py:134
  306.8 9.8 %select_reduce_fusion.1 = (f32[768]{0:T(1024)S(1)}, f32[768,1544]{0,1:T(8,128)}) fusion(pred[1544]{0:T(1024)(128)(4,1)S(1)} %broadcast_compare_fusion, bf16[768,2048]{1,0:T(8,128)(2,1)} %all-gather.9.cloned.1.call-done, bf16[1544,2048]{1,0:T(8,128)(2,1)} %reshape.285), kind=kOutput, calls=%fused_computation.23 | convolution fusion | flops 4860560384 | bytes 14217736 | tf_op jit(solution)/shard_map/dot_general | solution.py:146
  316.6 65.0 %pmax.7 = f32[768]{0:T(1024)S(1)} all-reduce(f32[768]{0:T(1024)S(1)} %get-tuple-element.53), channel_id=1, replica_groups=mesh['kv'=8,'z'=8,'y'=4] {'kv','y'}, use_global_device_ids=true, to_apply=%region_12.13 | all-reduce | flops 768 | bytes 6144 | tf_op jit(solution)/shard_map/pmax | solution.py:153
  381.6 4.5 multiply_reduce_fusion
  386.1 123.8 %all-reduce.1 = (f32[768]{0:T(1024)S(1)}, f32[768]{0:T(1024)S(1)}, f32[768]{0:T(1024)S(1)}) all-reduce(f32[768]{0:T(1024)S(1)} %get-tuple-element.37, f32[768]{0:T(1024)S(1)} %get-tuple-element.48, f32[768]{0:T(1024)S(1)} %get-tuple-element.47), channel_id=1, replica_groups=mesh['kv'=8,'z'=8,'y'=4] {'kv','y'}, use_global_device_ids=true, to_apply=%region_10.11 | all-reduce | flops 2304 | bytes 18432 | tf_op jit(solution)/shard_map/psum | solution.py:155
  (55 shorter events, 7.6 us)
Async XLA Ops:
  7.2 107.9 %copy-start = (bf16[256,2048]{1,0:T(8,128)(2,1)S(1)}, bf16[256,2048]{1,0:T(8,128)(2,1)}, u32[]{:S(2)}) copy-start(bf16[256,2048]{1,0:T(8,128)(2,1)} %param.18) | copy-start | bytes 3145732
  7.2 10.3 %copy-start.1 = (bf16[192,2048]{1,0:T(8,128)(2,1)S(1)}, bf16[192,2048]{1,0:T(8,128)(2,1)}, u32[]{:S(2)}) copy-start(bf16[192,2048]{1,0:T(8,128)(2,1)} %param.13) | copy-start | bytes 2359300
  7.2 10.3 %copy-start.5 = (f32[2048]{0:T(1024)S(1)}, f32[2048]{0:T(1024)}, u32[]{:S(2)}) copy-start(f32[2048]{0:T(1024)} %param.14) | copy-start | bytes 24580
  7.2 10.3 %copy-start.4 = (bf16[2048,256]{1,0:T(8,128)(2,1)S(1)}, bf16[2048,256]{1,0:T(8,128)(2,1)}, u32[]{:S(2)}) copy-start(bf16[2048,256]{1,0:T(8,128)(2,1)} %param.15) | copy-start | bytes 3145732
  7.2 86.5 %all-gather.7.cloned.1.call-start = ((), (), s32[]{:S(2)}) async-start(), calls=%async_computation | async-start | bytes 1622016 | tf_op jit(solution)/shard_map/all_gather | solution.py:87
  14.8 170.1 %all-gather.11.cloned.1.call-start = ((), (), s32[]{:S(2)}) async-start(), calls=%async_computation.2 | async-start | bytes 14155776 | tf_op jit(solution)/shard_map/all_gather | solution.py:131
  116.7 146.2 %all-gather.13.cloned.1.call-start = ((), (), s32[]{:S(2)}) async-start(), calls=%async_computation.3 | async-start | bytes 7372800 | tf_op jit(solution)/shard_map/all_gather | solution.py:136
  117.4 189.4 %all-gather.9.cloned.1.call-start = ((), (), s32[]{:S(2)}) async-start(), calls=%async_computation.1 | async-start | bytes 3932160 | tf_op jit(solution)/shard_map/all_gather | solution.py:134
  184.9 6.4 %copy-start.2 = (f32[2048]{0:T(1024)S(1)}, f32[2048]{0:T(1024)}, u32[]{:S(2)}) copy-start(f32[2048]{0:T(1024)} %param.19) | copy-start | bytes 24580
  190.9 1.8 copy-start.6
  190.9 3.8 copy-start.3
Sparse Core Ops, SparseCore 0:
  14.9 78.7 all-gather.6
  116.8 67.9 all-gather.10
  186.7 76.1 all-gather.12
  264.6 42.1 all-gather.8
